TPU v7x, 512 devices: a whole 4x8x8 slice. The times are simulated.
512 devices in a mesh: row: 16 (over z, core), col: 32 (over x, y).
Axes of the slice: x: 4, y: 8, z: 8, core: 2. Of those that a mesh axis runs over, the one named last changes fastest.
Arguments:
- pool: float32 [131072, 256], P(('row', 'col')), may hold values from -12 to 12
- row_pick: int32 [65536], replicated, may hold values from 0 to 8191, as said below
- length_scale: float32 [256], replicated, may hold values from 12 to 48
- panel_tile: int32 [1], replicated, may hold values from 0 to 959
Outputs:
- schur: float32 [65536, 4096], P('row', 'col')
- row_panel: float32 [65536, 64], P('row')
Inputs may be any that keep to these rules, and one draw needn't show every extreme that they name: `row_pick`: entry m indexes the 8192 pixels of tile-grid row m // 4096; entries of one tile-grid row are distinct, at most 160 of them lie in the 256 pixels of one device, and exactly 160 do for some device of each tile-grid row.
All inputs are finite; a program needn't handle non-finite values.
Results may differ from a plain program's by a relative error of at most 0.0003.
Values sent between devices are 32-bit elements; how exact they have to be, the bound alone decides.
No kernel may reach another device: no remote copies, remote signals or barrier semaphores. Data moves between devices by JAX's collectives and lax.ppermute only.
A program may use at most 64 MiB of HBM per device.

v0:
```python
import jax
import jax.numpy as jnp
from jax import lax
from jax.sharding import PartitionSpec as P

TB = 64
WT = 2
noise_level = 0.1
root_five = 5.0**0.5


def from_root(x, axis, root):
    mine = lax.axis_index(axis) == root
    return lax.psum(jnp.where(mine, x, jnp.zeros_like(x)), axis)


def kernel(left, right, left_index, right_index):
    left_sq = jnp.sum(left * left, axis=1)
    right_sq = jnp.sum(right * right, axis=1)
    cross = jnp.dot(
        left, right.T, precision=lax.Precision.HIGHEST, preferred_element_type=jnp.float32
    )
    dist_sq = jnp.maximum(left_sq[:, None] + right_sq[None, :] - 2.0 * cross, 0.0)
    radius = jnp.sqrt(dist_sq)
    value = (1.0 + root_five * radius + 5.0 / 3.0 * dist_sq) * jnp.exp(-root_five * radius)
    same = (left_index[:, None] == right_index[None, :]).astype(value.dtype)
    return value + noise_level * same


def panel_solve(factor, block):
    return lax.linalg.triangular_solve(factor, block, left_side=False, lower=True, transpose_a=True)


def body(pool, row_pick, length_scale, panel_tile):
    rows_count = lax.axis_size("row")
    cols_count = lax.axis_size("col")
    my_row = lax.axis_index("row")
    my_col = lax.axis_index("col")
    total_rows = row_pick.shape[0]
    local_rows = total_rows // rows_count
    my_pick = lax.dynamic_slice_in_dim(row_pick, my_row * local_rows, local_rows)
    gathered = lax.all_gather(pool, "col", axis=0, tiled=True)
    features = jnp.take(gathered, my_pick, axis=0)
    panel = panel_tile[0]
    tiles = panel + 1 + jnp.mod(my_col - panel - 1, cols_count) + cols_count * jnp.arange(WT)
    local_tiles = tiles // rows_count
    col_source = (local_tiles[:, None] * TB + jnp.arange(TB)[None, :]).reshape(-1)
    col_local = jnp.take(features, col_source, axis=0)
    col_feats = from_root(col_local, "row", my_col % rows_count)
    panel_row = panel % rows_count
    panel_local = panel // rows_count
    panel_rows = lax.dynamic_slice_in_dim(features, panel_local * TB, TB)
    panel_feats = from_root(panel_rows, "row", panel_row)
    inverse_scale = 1.0 / length_scale
    scaled_rows = features * inverse_scale
    scaled_cols = col_feats * inverse_scale
    scaled_panel = panel_feats * inverse_scale
    local_index = jnp.arange(local_rows)
    row_global = (local_index // TB * rows_count + my_row) * TB + local_index % TB
    col_global = (tiles[:, None] * TB + jnp.arange(TB)[None, :]).reshape(-1)
    panel_global = panel * TB + jnp.arange(TB)
    factor = jnp.linalg.cholesky(kernel(scaled_panel, scaled_panel, panel_global, panel_global))
    row_panel = panel_solve(factor, kernel(scaled_rows, scaled_panel, row_global, panel_global))
    col_panel = panel_solve(factor, kernel(scaled_cols, scaled_panel, col_global, panel_global))
    update = jnp.dot(
        row_panel, col_panel.T, precision=lax.Precision.HIGHEST, preferred_element_type=jnp.float32
    )
    schur = kernel(scaled_rows, scaled_cols, row_global, col_global) - update
    return (schur, row_panel)


def solution(mesh):
    in_specs = (P(("row", "col"), None), P(), P(), P())
    out_specs = (P("row", "col"), P("row", None))
    return jax.shard_map(body, mesh=mesh, in_specs=in_specs, out_specs=out_specs, check_vma=False)
```

profile of v0, /device:TPU:1, one launch (start us, length us, event | category | flops | bytes accessed | tf_op | source)
XLA Modules:
  0.0 298.0 jit_solution(12258355929983849131)
XLA Ops:
  7.2 0.0 all-gather.2.cloned.1.call-start
  7.2 0.7 all-gather.2.cloned.1.call-update
  7.9 0.0 all-reduce.3.cloned.1.call-start
  8.6 0.1 iota_add_fusion.1
  8.7 0.1 add.313
  8.8 0.1 add.310
  8.9 0.1 iota_add_fusion
  9.0 0.1 add.328
  9.1 0.7 compare_and_fusion
  9.8 0.7 fusion.75
  10.5 0.7 broadcast_divide_fusion
  11.2 107.6 %all-gather.2.cloned.1.call-done = f32[8192,256]{1,0:T(8,128)} async-done(((f32[256,256]{1,0:T(8,128)}), f32[8192,256]{1,0:T(8,128)}) %all-gather.2.cloned.1.call-update) | async-done | bytes 8388624 | tf_op jit(solution)/shard_map/all_gather | solution.py:42
  118.9 19.5 %gather_fusion = f32[4096,256]{1,0:T(8,128)} fusion(f32[8192,256]{1,0:T(8,128)} %all-gather.2.cloned.1.call-done, s32[4096]{0:T(1024)S(1)} %fusion.75), kind=kCustom, calls=%fused_computation | custom fusion | bytes 8404992 | tf_op jit(solution)/shard_map/jit(_take)/gather | solution.py:43
  138.3 4.1 %multiply_reduce_fusion = (f32[4096]{0:T(1024)S(1)}, f32[4096,256]{1,0:T(8,128)}) fusion(f32[256]{0:T(256)S(1)} %broadcast_divide_fusion, f32[4096,256]{1,0:T(8,128)} %gather_fusion, pred[4096]{0:T(1024)(128)(4,1)S(1)} %compare_and_fusion), kind=kLoop, calls=%fused_computation.9 | loop fusion | flops 4190208 | bytes 8410112 | tf_op jit(solution)/shard_map/reduce_sum | solution.py:18
  142.4 2.9 gather_fusion.1
  145.4 1.5 dynamic-slice_select_fusion
  146.8 0.7 select_select_fusion
  147.6 0.0 all-reduce.3.cloned.1.call-update
  147.6 110.7 %all-reduce.3.cloned.1.call-done = (f32[64,256]{1,0:T(8,128)}, f32[128,256]{1,0:T(8,128)}) async-done(((f32[64,256]{1,0:T(8,128)}, f32[128,256]{1,0:T(8,128)}), (f32[64,256]{1,0:T(8,128)}, f32[128,256]{1,0:T(8,128)})) %all-reduce.3.cloned.1.call-update) | async-done | bytes 196624 | tf_op jit(solution)/shard_map/psum | solution.py:14
  258.3 0.9 multiply_reduce_fusion.2
  259.3 1.1 fusion.91
  260.4 0.0 copy-start.1
  260.4 0.0 copy-start.2
  260.5 0.0 copy-start
  260.5 6.6 %fusion.3 = f32[4096,64]{0,1:T(8,128)S(1)} fusion(f32[4096,256]{1,0:T(8,128)} %get-tuple-element.7, f32[256]{0:T(256)S(1)} %broadcast_divide_fusion, f32[64]{0:T(128)S(1)} %multiply_reduce_fusion.2, f32[4096]{0:T(1024)S(1)} %get-tuple-element.6, f32[64,256]{1,0:T(8,128)} %get-tuple-element.2), kind=kOutput, calls=%fused_computation.8 | convolution fusion | flops 807419904 | bytes 5326080 | tf_op jit(solution)/shard_map/dot_general | solution.py:20
  267.1 0.0 copy-done.1
  267.1 0.1 multiply_reduce_fusion.1
  267.2 0.0 copy-done.2
  267.2 0.3 fusion.9
  267.5 0.0 copy-done
  267.5 3.4 %fusion.1 = f32[4096,128]{1,0:T(8,128)S(1)} fusion(f32[4096,256]{1,0:T(8,128)S(1)} %copy-done, f32[256]{0:T(256)S(1)} %broadcast_divide_fusion, f32[128]{0:T(128)S(1)} %multiply_reduce_fusion.1, f32[4096]{0:T(1024)S(1)} %get-tuple-element.6, f32[128,256]{1,0:T(8,128)S(1)} %copy-done.1), kind=kOutput, calls=%fused_computation.5 | convolution fusion | flops 1613791232 | bytes 6440448 | tf_op jit(solution)/shard_map/dot_general | solution.py:20
  270.9 0.1 copy.8
  271.0 0.1 copy.9
  271.1 0.1 copy.6
  271.2 0.1 add_multiply_fusion
  271.3 5.8 %cholesky.15 = f32[64,64]{1,0:T(8,128)S(1)} custom-call(f32[64,64]{1,0:T(8,128)S(1)} %add_multiply_fusion), custom_call_target="Cholesky" | custom-call | tf_op jit(solution)/shard_map/jit(cholesky)/cholesky | solution.py:62
  277.2 0.6 compare_reduce_fusion
  277.8 0.7 fusion.37
  278.5 4.9 %custom-call.8 = f32[1,64,64]{1,2,0:T(8,128)S(1)} custom-call(f32[1,64,64]{2,1,0:T(8,128)S(1)} %fusion.37), custom_call_target="InvertDiagBlocksLowerTriangular" | custom-call | tf_op jit(solution)/shard_map/triangular_solve | solution.py:31
  283.4 1.7 fusion.10
  285.1 0.0 copy-start.3
  285.1 0.4 fusion.38
  285.5 5.7 %convolution_subtract_fusion = f32[4096,128]{1,0:T(8,128)} fusion(f32[4096,64]{0,1:T(8,128)S(1)} %fusion.10, f32[128,64]{1,0:T(8,128)S(1)} %fusion.38, f32[4096,128]{1,0:T(8,128)S(1)} %fusion.1, s32[128]{0:T(128)S(1)} %add.328, s32[4096]{0:T(1024)S(1)} %fusion.65), kind=kOutput, calls=%fused_computation.2 | convolution fusion | flops 407896064 | bytes 5292544 | tf_op jit(solution)/shard_map/dot_general | solution.py:65
  291.1 0.0 copy-done.3
  (7 shorter events, 0.1 us)
Async XLA Ops:
  7.2 111.7 %all-gather.2.cloned.1.call-start = ((), (), s32[]{:S(2)}) async-start(), calls=%async_computation | async-start | bytes 8650752 | tf_op jit(solution)/shard_map/all_gather | solution.py:42
  7.9 250.4 %all-reduce.3.cloned.1.call-start = ((), (), s32[]{:S(2)}) async-start(), calls=%async_computation.1 | async-start | bytes 393216 | tf_op jit(solution)/shard_map/psum | solution.py:14
  260.4 6.7 %copy-start.1 = (f32[128,256]{1,0:T(8,128)S(1)}, f32[128,256]{1,0:T(8,128)}, u32[]{:S(2)}) copy-start(f32[128,256]{1,0:T(8,128)} %get-tuple-element.3) | copy-start | bytes 393220
  260.4 6.8 %copy-start.2 = (f32[64,256]{1,0:T(8,128)S(1)}, f32[64,256]{1,0:T(8,128)}, u32[]{:S(2)}) copy-start(f32[64,256]{1,0:T(8,128)} %get-tuple-element.2) | copy-start | bytes 196612
  260.5 7.0 %copy-start = (f32[4096,256]{1,0:T(8,128)S(1)}, f32[4096,256]{1,0:T(8,128)}, u32[]{:S(2)}) copy-start(f32[4096,256]{1,0:T(8,128)} %get-tuple-element.7) | copy-start | bytes 12582916
  285.1 6.0 %copy-start.3 = (f32[4096,64]{0,1:T(8,128)}, f32[4096,64]{0,1:T(8,128)S(1)}, u32[]{:S(2)}) copy-start(f32[4096,64]{0,1:T(8,128)S(1)} %fusion.10) | copy-start | bytes 3145732
Sparse Core Ops, SparseCore 0:
  11.1 107.6 all-gather.1
  147.7 110.5 all-reduce.2
where the time goes:
time: 298 us
  waiting for transfers between devices  219 us (73%)
  local copies, waits for them, and re-layouts  22.9 us (8%)
  other arithmetic  21.9 us (7%)
  matrix products  19.2 us (6%)
  between operations  14.9 us (5%)
    psum x1, waiting for transfers between devices, from_root(): return lax.psum(jnp.where(mine, x, jnp.zeros_like(x)), axis)  111 us
    all_gather x1, waiting for transfers between devices, body(): gathered = lax.all_gather(pool, 'col', axis=0, tiled=True)  108 us
    gather x1, local copies, waits for them, and re-layouts, body(): features = jnp.take(gathered, my_pick, axis=0)  19.5 us
    dot_general x4, matrix products, kernel(): jnp.dot(left, right.T, precision=lax.Precision.HIGHEST, preferred_element...  11.5 us
    another operation x3, other arithmetic, body(): jnp.linalg.cholesky(kernel(scaled_panel, scaled_panel, panel_global, pane...  6.52 us
  transfers between devices with their start and end apart: 2, of which 2 were waited for; matrix products, arithmetic and copies ran while one was open for 1% of the time, Pallas kernels for 0%

commit v1 on v0

--- a/solution.py
+++ b/solution.py
@@ -39,7 +39,9 @@
     total_rows = row_pick.shape[0]
     local_rows = total_rows // rows_count
     my_pick = lax.dynamic_slice_in_dim(row_pick, my_row * local_rows, local_rows)
-    gathered = lax.all_gather(pool, "col", axis=0, tiled=True)
+    gathered = jnp.concatenate(
+        lax.all_to_all(jnp.stack([pool] * lax.axis_size("col")), "col", 0, 0), axis=0
+    )
     features = jnp.take(gathered, my_pick, axis=0)
     panel = panel_tile[0]
     tiles = panel + 1 + jnp.mod(my_col - panel - 1, cols_count) + cols_count * jnp.arange(WT)

time: 298 us -> 398 us (1.34)
  waiting for transfers between devices: 219 us -> 304 us
  starting transfers between devices: 0.08 us -> 10.8 us
  local copies, waits for them, and re-layouts: 22.9 us -> 28 us
    all_to_all x0 -> x1, waiting for transfers between devices: none -> 181 us  [body(): lax.all_to_all(jnp.stack([pool] * lax.axis_size('col')), 'col', 0, 0)]
    all_gather x1 -> x0, waiting for transfers between devices: 108 us -> none  [body(): gathered = lax.all_gather(pool, 'col', axis=0, tiled=True)]
    psum x1, waiting for transfers between devices: 111 us -> 123 us  [from_root(): return lax.psum(jnp.where(mine, x, jnp.zeros_like(x)), axis)]
    all_to_all x0 -> x1, starting transfers between devices: none -> 10.7 us  [body(): lax.all_to_all(jnp.stack([pool] * lax.axis_size('col')), 'col', 0, 0)]
    another operation x0 -> x1, local copies, waits for them, and re-layouts: none -> 5.11 us  [body(): jnp.stack([pool] * lax.axis_size('col'))]
  transfers between devices with their start and end apart: 2 -> 2, of which waited for: 2 -> 2; matrix products, arithmetic and copies ran while one was open for 1% -> 0% of each run, Pallas kernels for 0% -> 0%
where the time goes in v1:
time: 398 us
  waiting for transfers between devices  304 us (76%)
  local copies, waits for them, and re-layouts  28 us (7%)
  other arithmetic  21.2 us (5%)
  matrix products  19.2 us (5%)
  between operations  14.9 us (4%)
  starting transfers between devices  10.8 us (3%)
    all_to_all x1, waiting for transfers between devices, body(): lax.all_to_all(jnp.stack([pool] * lax.axis_size('col')), 'col', 0, 0)  181 us
    psum x1, waiting for transfers between devices, from_root(): return lax.psum(jnp.where(mine, x, jnp.zeros_like(x)), axis)  123 us
    gather x1, local copies, waits for them, and re-layouts, body(): features = jnp.take(gathered, my_pick, axis=0)  19.5 us
    dot_general x4, matrix products, kernel(): jnp.dot(left, right.T, precision=lax.Precision.HIGHEST, preferred_element...  11.5 us
    all_to_all x1, starting transfers between devices, body(): lax.all_to_all(jnp.stack([pool] * lax.axis_size('col')), 'col', 0, 0)  10.7 us
  transfers between devices with their start and end apart: 2, of which 2 were waited for; matrix products, arithmetic and copies ran while one was open for 0% of the time, Pallas kernels for 0%

profile of v1, /device:TPU:1, one launch (start us, length us, event | category | flops | bytes accessed | tf_op | source)
XLA Modules:
  0.0 397.9 jit_solution(2808629964894247682)
XLA Ops:
  7.2 5.1 %stack.2 = f32[32,256,256]{2,1,0:T(8,128)} broadcast(f32[256,256]{1,0:T(8,128)} %param.4), dimensions={1,2} | broadcast | bytes 8650752 | tf_op jit(solution)/shard_map/stack | solution.py:43
  12.3 0.0 copy-start.3
  12.3 10.7 %all-to-all-start = ((f32[32,256,256]{2,1,0:T(8,128)}), f32[32,256,256]{2,1,0:T(8,128)}, u32[]{:S(2)}, u32[]{:S(2)}) async-start(f32[32,256,256]{2,1,0:T(8,128)} %stack.2), calls=%async_computation | async-start | bytes 16777216 | tf_op jit(solution)/shard_map/all_to_all | solution.py:43
  23.0 0.0 all-reduce.3.cloned.1.call-start
  23.8 0.1 iota_add_fusion.1
  23.9 0.1 add.313
  23.9 0.1 add.310
  24.0 0.1 iota_add_fusion
  24.1 0.1 add.328
  24.2 0.7 compare_and_fusion
  24.9 0.7 fusion.75
  25.7 0.0 copy-done.3
  25.7 181.0 %all-to-all-done = f32[32,256,256]{2,1,0:T(8,128)} async-done(((f32[32,256,256]{2,1,0:T(8,128)}), f32[32,256,256]{2,1,0:T(8,128)}, u32[]{:S(2)}, u32[]{:S(2)}) %all-to-all-start) | async-done | bytes 8388640 | tf_op jit(solution)/shard_map/all_to_all | solution.py:43
  206.7 19.5 %gather_fusion = f32[4096,256]{1,0:T(8,128)} fusion(f32[8192,256]{1,0:T(8,128)} %bitcast, s32[4096]{0:T(1024)S(1)} %fusion.75), kind=kCustom, calls=%fused_computation | custom fusion | bytes 8404992 | tf_op jit(solution)/shard_map/jit(_take)/gather | solution.py:45
  226.1 4.1 %multiply_reduce_fusion = (f32[4096]{0:T(1024)S(1)}, f32[4096,256]{1,0:T(8,128)}) fusion(f32[256]{0:T(256)S(1)} %broadcast_divide_fusion, f32[4096,256]{1,0:T(8,128)} %gather_fusion, pred[4096]{0:T(1024)(128)(4,1)S(1)} %compare_and_fusion), kind=kLoop, calls=%fused_computation.9 | loop fusion | flops 4190208 | bytes 8410112 | tf_op jit(solution)/shard_map/reduce_sum | solution.py:18
  230.2 2.9 gather_fusion.1
  233.2 1.5 dynamic-slice_select_fusion
  234.7 0.7 select_select_fusion
  235.4 0.0 all-reduce.3.cloned.1.call-update
  235.5 122.8 %all-reduce.3.cloned.1.call-done = (f32[64,256]{1,0:T(8,128)}, f32[128,256]{1,0:T(8,128)}) async-done(((f32[64,256]{1,0:T(8,128)}, f32[128,256]{1,0:T(8,128)}), (f32[64,256]{1,0:T(8,128)}, f32[128,256]{1,0:T(8,128)})) %all-reduce.3.cloned.1.call-update) | async-done | bytes 196624 | tf_op jit(solution)/shard_map/psum | solution.py:14
  358.3 0.9 multiply_reduce_fusion.2
  359.2 1.1 fusion.91
  360.4 0.0 copy-start.1
  360.4 0.0 copy-start.2
  360.4 0.0 copy-start
  360.4 6.6 %fusion.3 = f32[4096,64]{0,1:T(8,128)S(1)} fusion(f32[4096,256]{1,0:T(8,128)} %get-tuple-element.7, f32[256]{0:T(256)S(1)} %broadcast_divide_fusion, f32[64]{0:T(128)S(1)} %multiply_reduce_fusion.2, f32[4096]{0:T(1024)S(1)} %get-tuple-element.6, f32[64,256]{1,0:T(8,128)} %get-tuple-element.2), kind=kOutput, calls=%fused_computation.8 | convolution fusion | flops 807419904 | bytes 5326080 | tf_op jit(solution)/shard_map/dot_general | solution.py:20
  367.1 0.0 copy-done.1
  367.1 0.1 multiply_reduce_fusion.1
  367.2 0.0 copy-done.2
  367.2 0.3 fusion.9
  367.4 0.0 copy-done
  367.5 3.4 fusion.1
  370.9 0.1 copy.8
  371.0 0.1 copy.9
  371.0 0.1 copy.6
  371.1 0.1 add_multiply_fusion
  371.2 5.8 %cholesky.15 = f32[64,64]{1,0:T(8,128)S(1)} custom-call(f32[64,64]{1,0:T(8,128)S(1)} %add_multiply_fusion), custom_call_target="Cholesky" | custom-call | tf_op jit(solution)/shard_map/jit(cholesky)/cholesky | solution.py:64
  377.1 0.6 compare_reduce_fusion
  377.8 0.7 fusion.37
  378.4 4.9 %custom-call.8 = f32[1,64,64]{1,2,0:T(8,128)S(1)} custom-call(f32[1,64,64]{2,1,0:T(8,128)S(1)} %fusion.37), custom_call_target="InvertDiagBlocksLowerTriangular" | custom-call | tf_op jit(solution)/shard_map/triangular_solve | solution.py:31
  383.3 1.7 fusion.10
  385.0 0.0 copy-start.4
  385.1 0.4 fusion.38
  385.4 5.7 %convolution_subtract_fusion = f32[4096,128]{1,0:T(8,128)} fusion(f32[4096,64]{0,1:T(8,128)S(1)} %fusion.10, f32[128,64]{1,0:T(8,128)S(1)} %fusion.38, f32[4096,128]{1,0:T(8,128)S(1)} %fusion.1, s32[128]{0:T(128)S(1)} %add.328, s32[4096]{0:T(1024)S(1)} %fusion.65), kind=kOutput, calls=%fused_computation.2 | convolution fusion | flops 407896064 | bytes 5292544 | tf_op jit(solution)/shard_map/dot_general | solution.py:67
  391.1 0.0 copy-done.4
  (8 shorter events, 0.1 us)
Async XLA Ops:
  12.3 13.4 %copy-start.3 = (f32[256]{0:T(256)S(1)}, f32[256]{0:T(256)}, u32[]{:S(2)}) copy-start(f32[256]{0:T(256)} %param.6) | copy-start | bytes 3076
  12.3 194.4 %all-to-all-start = ((f32[32,256,256]{2,1,0:T(8,128)}), f32[32,256,256]{2,1,0:T(8,128)}, u32[]{:S(2)}, u32[]{:S(2)}) async-start(f32[32,256,256]{2,1,0:T(8,128)} %stack.2), calls=%async_computation | async-start | bytes 16777216 | tf_op jit(solution)/shard_map/all_to_all | solution.py:43
  23.0 335.3 %all-reduce.3.cloned.1.call-start = ((), (), s32[]{:S(2)}) async-start(), calls=%async_computation.1 | async-start | bytes 393216 | tf_op jit(solution)/shard_map/psum | solution.py:14
  360.4 6.7 %copy-start.1 = (f32[128,256]{1,0:T(8,128)S(1)}, f32[128,256]{1,0:T(8,128)}, u32[]{:S(2)}) copy-start(f32[128,256]{1,0:T(8,128)} %get-tuple-element.3) | copy-start | bytes 393220
  360.4 6.8 %copy-start.2 = (f32[64,256]{1,0:T(8,128)S(1)}, f32[64,256]{1,0:T(8,128)}, u32[]{:S(2)}) copy-start(f32[64,256]{1,0:T(8,128)} %get-tuple-element.2) | copy-start | bytes 196612
  360.4 7.0 %copy-start = (f32[4096,256]{1,0:T(8,128)S(1)}, f32[4096,256]{1,0:T(8,128)}, u32[]{:S(2)}) copy-start(f32[4096,256]{1,0:T(8,128)} %get-tuple-element.7) | copy-start | bytes 12582916
  385.0 6.0 %copy-start.4 = (f32[4096,64]{0,1:T(8,128)}, f32[4096,64]{0,1:T(8,128)S(1)}, u32[]{:S(2)}) copy-start(f32[4096,64]{0,1:T(8,128)S(1)} %fusion.10) | copy-start | bytes 3145732
Sparse Core Ops, SparseCore 0:
  235.6 122.6 all-reduce.2
